TPU v7x, 256 devices: a whole 4x4x8 slice. The times are simulated.
256 devices in a mesh: lat: 8 (over z), lev: 32 (over x, y, core).
Axes of the slice: x: 4, y: 4, z: 8, core: 2. Of those that a mesh axis runs over, the one named last changes fastest.
Arguments:
- spec_in: bfloat16 [32, 640, 1281], P('lev', 'lat'), may hold values from -6 to 6
- legendre: bfloat16 [640, 1280, 1281], P('lat', 'lev'), may hold values from -0.15625 to 0.15625
- gauss_weights: float32 [1280], P('lev'), may hold values from 0.1 to 1
- row_points: int32 [2, 1280], P(None, 'lev'), may hold values from 4 to 5120
Outputs:
- spec_out: bfloat16 [32, 640, 1281], P('lev', 'lat')
All inputs are finite; a program needn't handle non-finite values.
Results may differ from a plain program's by a relative error of at most 0.02.
Values may be sent and summed in bfloat16 or wider, within the bound.
No kernel may reach another device: no remote copies, remote signals or barrier semaphores. Data moves between devices by JAX's collectives and lax.ppermute only.
A program may use at most 128 MiB of HBM per device.

v0:
```python
import math
import jax
import jax.numpy as jnp
from jax import lax
from jax.sharding import PartitionSpec as P

NLON = 5120
SLOT_CODES = (0, 0, 1, 1)
PARITY_CODES = (0, 1, 0, 1)


def pair_masks(first_pair, pair_count, packed):
    pair_ids = first_pair + jnp.arange(pair_count, dtype=jnp.int32)
    positions = jnp.arange(packed, dtype=jnp.int32)
    boundary = packed - 1 - pair_ids
    in_second = (positions[None, :] >= boundary[:, None]).astype(jnp.int32)
    degree = positions[None, :] - in_second * boundary[:, None]
    parity = degree % 2
    slot_codes = jnp.array(SLOT_CODES, dtype=jnp.int32)
    parity_codes = jnp.array(PARITY_CODES, dtype=jnp.int32)
    return (in_second[:, :, None] == slot_codes) & (parity[:, :, None] == parity_codes)


def wave_tables(total_pairs, truncation):
    pair_ids = jnp.arange(total_pairs, dtype=jnp.int32)
    wavenumbers = jnp.stack([pair_ids, truncation - pair_ids], axis=1)
    longitudes = jnp.arange(NLON, dtype=jnp.int32)
    phases = wavenumbers[:, :, None] * longitudes[None, None, :] % NLON
    angles = phases.astype(jnp.float32) * (2.0 * math.pi / NLON)
    return (jnp.cos(angles).astype(jnp.bfloat16), jnp.sin(angles).astype(jnp.bfloat16), wavenumbers)


def fourier_work(spectrum, row_counts, cosines, sines, wavenumbers, truncation):
    kept_mask = (2 * wavenumbers[:, None, :] < row_counts[None, :, None]).astype(jnp.float32)
    masked = spectrum * kept_mask[..., None].astype(jnp.bfloat16)
    half_channels = spectrum.shape[-1] // 2
    levels = half_channels // 2
    real_part = masked[..., :half_channels]
    imag_part = masked[..., half_channels:]
    grid_values = jnp.einsum(
        "plsf,psk->lfk", real_part, cosines, preferred_element_type=jnp.float32
    )
    grid_values = (
        grid_values
        - jnp.einsum("plsf,psk->lfk", imag_part, sines, preferred_element_type=jnp.float32)
    ) * (1.0 / math.sqrt(truncation + 1))
    vortex = grid_values[:, :levels]
    divergence = grid_values[:, levels:]
    products = jnp.concatenate(
        [vortex * divergence, 0.5 * (vortex * vortex - divergence * divergence)], axis=1
    ).astype(jnp.bfloat16)
    scale_back = 4.0 / math.sqrt(NLON)
    real_out = (
        jnp.einsum("lfk,psk->plsf", products, cosines, preferred_element_type=jnp.float32)
        * scale_back
    )
    imag_out = (
        -jnp.einsum("lfk,psk->plsf", products, sines, preferred_element_type=jnp.float32)
        * scale_back
    )
    return (jnp.concatenate([real_out, imag_out], axis=-1) * kept_mask[..., None]).astype(
        jnp.bfloat16
    )


def local(spec_in, legendre, gauss_weights, row_points):
    pair_count, lat_count, packed = legendre.shape
    truncation = packed - 2
    groups = lax.axis_size("lat")
    local_channels = spec_in.shape[0]
    channels = local_channels * lax.axis_size("lev")
    tile_size = math.gcd(pair_count, 8)
    tile_count = pair_count // tile_size
    first_pair = lax.axis_index("lat") * pair_count
    selector = pair_masks(first_pair, pair_count, packed)
    select_half = selector.astype(jnp.bfloat16).reshape(tile_count, tile_size, packed, 4)
    select_full = selector.astype(jnp.float32).reshape(tile_count, tile_size, packed, 4)
    legendre_tiles = legendre.reshape(tile_count, tile_size, lat_count, packed)
    gathered = lax.all_gather(spec_in, "lev", axis=0, tiled=True)
    piece_width = gathered.shape[0]
    spectral = jnp.moveaxis(gathered.reshape(piece_width, tile_count, tile_size, packed), 1, 0)

    def inverse_tile(inputs):
        legendre_tile, spectral_tile, select_tile = inputs
        spread = spectral_tile[None] * jnp.moveaxis(select_tile, 2, 0)[:, None]
        return jnp.einsum(
            "pjq,xcpq->pjxc", legendre_tile, spread, preferred_element_type=jnp.float32
        )

    tile_sums = lax.map(inverse_tile, (legendre_tiles, spectral, select_half))
    legendre_sums = tile_sums.reshape(pair_count, lat_count, 4, piece_width)
    even_part = legendre_sums[:, :, 0::2]
    odd_part = legendre_sums[:, :, 1::2]
    fourier = jnp.concatenate([even_part + odd_part, even_part - odd_part], axis=1).astype(
        jnp.bfloat16
    )
    cosines, sines, wavenumbers = wave_tables(pair_count * groups, truncation)
    local_rows = row_points.reshape(1, 2 * lat_count)
    band_lats = 2 * lat_count // groups
    lat_rows = lax.all_to_all(fourier, "lat", split_axis=1, concat_axis=0, tiled=True)
    my_rows = lax.dynamic_slice_in_dim(local_rows[0], lax.axis_index("lat") * band_lats, band_lats)
    answered = fourier_work(lat_rows, my_rows, cosines, sines, wavenumbers, truncation)
    answered = answered.reshape(groups, pair_count, band_lats, 2, channels)
    returned = lax.all_to_all(answered, "lat", split_axis=0, concat_axis=0, tiled=True)
    back = jnp.moveaxis(returned, 0, 1).reshape(pair_count, 2 * lat_count, 2, channels)
    north_rows = back[:, :lat_count].astype(jnp.float32)
    south_rows = back[:, lat_count:].astype(jnp.float32)
    weights = gauss_weights[None, :, None, None]
    weighted = jnp.stack(
        [weights * (north_rows + south_rows), weights * (north_rows - south_rows)], axis=3
    )
    weighted = weighted.reshape(pair_count, lat_count, 4, channels).astype(jnp.bfloat16)
    part_tiles = weighted.reshape(
        tile_count, tile_size, lat_count, 4, local_channels * lax.axis_size("lev")
    )

    def direct_tile(inputs):
        legendre_tile, weighted_tile, select_tile = inputs
        full_sums = jnp.einsum(
            "pjq,pjxc->pqxc", legendre_tile, weighted_tile, preferred_element_type=jnp.float32
        )
        picked = jnp.sum(full_sums * select_tile[:, :, :, None], axis=2)
        return jnp.moveaxis(picked, 2, 0)

    picked_tiles = lax.map(direct_tile, (legendre_tiles, part_tiles, select_full))
    return lax.psum_scatter(
        jnp.moveaxis(picked_tiles, 0, 1)
        .reshape(local_channels * lax.axis_size("lev"), pair_count, packed)
        .astype(jnp.bfloat16),
        "lev",
        scatter_dimension=0,
        tiled=True,
    )


def solution(mesh):
    return jax.shard_map(
        local,
        mesh=mesh,
        in_specs=(P("lev", "lat", None), P("lat", "lev", None), P("lev"), P(None, "lev")),
        out_specs=P("lev", "lat", None),
        check_vma=False,
    )
```

profile of v0, /device:TPU:2, one launch (start us, length us, event | category | flops | bytes accessed | tf_op | source)
XLA Modules:
  0.0 796.2 jit_solution(10550959991378505809)
XLA Ops:
  7.7 2.7 fusion.74
  10.4 57.7 %all-gather.2.cloned.1.call-done = bf16[32,80,1281]{2,1,0:T(8,128)(2,1)} async-done(((bf16[1,80,1281]{2,1,0:T(8,128)(2,1)}), bf16[32,80,1281]{2,1,0:T(8,128)(2,1)}) %all-gather.2.cloned.1.call-update) | async-done | bytes 6558736 | tf_op jit(solution)/shard_map/all_gather | solution.py:79
  68.2 7.5 copy.45
  75.6 45.0 %while.20 = (s32[]{:T(128)}, f32[10,8,40,4,32]{2,4,3,1,0:T(8,128)}, bf16[10,8,40,1281]{3,2,1,0:T(8,128)(2,1)}, bf16[10,32,8,1281]{3,1,2,0:T(8,128)(2,1)}, bf16[10,8,1281,4]{2,3,1,0:T(4,128)(2,1)S(1)}, /*index=5*/s32[]{:T(128)}) while((s32[]{:T(128)}, f32[10,8,40,4,32]{2,4,3,1,0:T(8,128)}, bf16[10,8,40,1281]{3,2,1,0:T(8,128)(2,1)}, ...), condition=%wide.region_1.2_spmd, body=%wide.region_0.1_spmd.sunk | while | flops 106251264 | bytes 9575181 | solution.py:90
  75.6 1.2 dynamic-slice_bitcast_fusion.7
  77.2 2.1 fusion.110
  80.1 1.2 dynamic-slice_bitcast_fusion.7
  81.7 2.1 fusion.110
  84.6 1.2 dynamic-slice_bitcast_fusion.7
  86.2 2.1 fusion.110
  89.1 1.2 dynamic-slice_bitcast_fusion.7
  90.7 2.1 fusion.110
  93.6 1.2 dynamic-slice_bitcast_fusion.7
  95.2 2.1 fusion.110
  98.1 1.2 dynamic-slice_bitcast_fusion.7
  99.6 2.1 fusion.110
  102.6 1.2 dynamic-slice_bitcast_fusion.7
  104.2 2.1 fusion.110
  107.1 1.2 dynamic-slice_bitcast_fusion.7
  108.7 2.1 fusion.110
  111.6 1.2 dynamic-slice_bitcast_fusion.7
  113.2 2.1 fusion.110
  116.1 1.2 dynamic-slice_bitcast_fusion.7
  117.7 2.1 fusion.110
  120.6 3.4 add_convert_fusion
  124.7 3.5 copy.32
  128.2 7.0 all-to-all-start
  135.6 34.4 %all-to-all-done = bf16[80,80,2,32]{0,3,2,1:T(8,128)(2,1)S(1)} async-done(((bf16[80,80,2,32]{0,3,2,1:T(8,128)(2,1)}), bf16[80,80,2,32]{0,3,2,1:T(8,128)(2,1)S(1)}, u32[]{:S(2)}, u32[]{:S(2)}) %all-to-all-start) | async-done | bytes 819232 | tf_op jit(solution)/shard_map/all_to_all | solution.py:100
  170.0 1.0 copy.33
  171.0 1.0 all_to_all.19
  172.2 103.9 %fusion.27 = f32[10,16,5120]{2,1,0:T(8,128)S(1)} fusion(s32[640,2]{0,1:T(2,128)S(1)} %get-tuple-element.90, bf16[640,10,2,16]{0,3,2,1:T(8,128)(2,1)S(1)} %fusion.96), kind=kOutput, calls=%fused_computation.38 | convolution fusion | flops 2162688000 | bytes 3691520 | tf_op jit(solution)/shard_map/plsf,psk->lfk/dot_general | solution.py:45
  276.1 103.4 %fusion.30 = f32[10,16,5120]{2,1,0:T(8,128)S(1)} fusion(f32[10,16,5120]{2,1,0:T(8,128)S(1)} %fusion.27, s32[640,2]{0,1:T(2,128)S(1)} %get-tuple-element.90, bf16[640,10,2,16]{0,3,2,1:T(8,128)(2,1)S(1)} %fusion.98), kind=kOutput, calls=%fused_computation.39 | convolution fusion | flops 2164326400 | bytes 6968320 | tf_op jit(solution)/shard_map/plsf,psk->lfk/dot_general | solution.py:40
  380.0 1.3 maximum_bitcast_fusion.10
  381.3 103.4 %fusion.41 = f32[640,10,2,16]{0,3,1,2:T(8,128)S(1)} fusion(s32[640,2]{0,1:T(2,128)S(1)} %get-tuple-element.90, bf16[10,16,5120,1]{2,1,0,3:T(8,128)(2,1)S(1)} %maximum_bitcast_fusion.9), kind=kOutput, calls=%fused_computation.57 | convolution fusion | flops 2162892800 | bytes 2462720 | tf_op jit(solution)/shard_map/lfk,psk->plsf/dot_general | solution.py:54
  485.5 107.6 %fusion.50 = f32[640,10,2,16]{0,3,1,2:T(8,128)S(1)} fusion(s32[640,2]{0,1:T(2,128)S(1)} %get-tuple-element.90, bf16[10,16,5120,1]{2,1,0,3:T(8,128)(2,1)} %maximum_bitcast_fusion.10), kind=kOutput, calls=%fused_computation.60 | convolution fusion | flops 2163097600 | bytes 2462720 | tf_op jit(solution)/shard_map/lfk,psk->plsf/dot_general | solution.py:58
  594.0 1.6 fusion.33
  595.6 3.6 all-to-all-start.1
  599.2 34.7 %all-to-all-done.1 = bf16[8,80,10,2,32]{1,4,3,2,0:T(8,128)(2,1)S(1)} async-done(((bf16[8,80,10,2,32]{1,4,3,2,0:T(8,128)(2,1)}), bf16[8,80,10,2,32]{1,4,3,2,0:T(8,128)(2,1)S(1)}, u32[]{:S(2)}, u32[]{:S(2)}) %all-to-all-start.1) | async-done | bytes 819232 | tf_op jit(solution)/shard_map/all_to_all | solution.py:104
  634.3 1.4 pad_maximum_fusion.1
  635.7 5.9 copy.36
  641.6 46.5 %while.21 = (s32[]{:T(128)}, bf16[10,32,8,1281]{3,1,2,0:T(8,128)(2,1)}, bf16[10,8,40,1281]{3,2,1,0:T(8,128)(2,1)}, bf16[10,8,40,4,32]{2,4,3,1,0:T(8,128)(2,1)S(1)}, f32[10,8,1281,4]{2,3,1,0:T(4,128)}, /*index=5*/s32[]{:T(128)}) while((s32[]{:T(128)}, bf16[10,32,8,1281]{3,1,2,0:T(8,128)(2,1)}, bf16[10,8,40,1281]{3,2,1,0:T(8,128)(2,1)}, ...), condition=%wide.region_4.5_spmd, body=%wide.region_2.4_spmd.sunk | while | flops 107235072 | bytes 14686669 | solution.py:125
  641.7 2.1 fusion.113
  643.8 0.9 dynamic-slice_bitcast_fusion.8
  646.3 2.1 fusion.113
  648.4 0.9 dynamic-slice_bitcast_fusion.8
  651.0 2.1 fusion.113
  653.0 0.9 dynamic-slice_bitcast_fusion.8
  655.6 2.1 fusion.113
  657.7 0.9 dynamic-slice_bitcast_fusion.8
  660.3 2.1 fusion.113
  662.3 0.9 dynamic-slice_bitcast_fusion.8
  664.9 2.1 fusion.113
  667.0 0.9 dynamic-slice_bitcast_fusion.8
  669.6 2.1 fusion.113
  671.6 0.9 dynamic-slice_bitcast_fusion.8
  674.2 2.1 fusion.113
  676.3 0.9 dynamic-slice_bitcast_fusion.8
  677.9 1.0 bitcast_dynamic-update-slice_fusion.2
  678.9 2.1 fusion.113
  680.9 0.9 dynamic-slice_bitcast_fusion.8
  683.5 2.1 fusion.113
  685.6 0.9 dynamic-slice_bitcast_fusion.8
  688.1 8.4 %copy.44 = bf16[32,10,8,1281]{3,2,1,0:T(8,128)(2,1)} copy(bf16[32,10,8,1281]{3,0,2,1:T(8,128)(2,1)} %bitcast.110) | data formatting | bytes 13117440 | tf_op jit(solution)/shard_map/convert_element_type | solution.py:129
  696.6 92.5 %reduce-scatter.2.cloned.1.call-done = bf16[1,80,1281]{2,1,0:T(8,128)(2,1)} async-done(((bf16[32,80,1281]{2,1,0:T(8,128)(2,1)}), bf16[1,80,1281]{2,1,0:T(8,128)(2,1)}) %reduce-scatter.2.cloned.1.call-update) | async-done | bytes 204976 | tf_op jit(solution)/shard_map/reduce_scatter | solution.py:126
  (92 shorter events, 32.8 us)
Async XLA Ops:
  6.5 61.6 %all-gather.2.cloned.1.call-start = ((), (), s32[]{:S(2)}) async-start(), calls=%async_computation.3 | async-start | bytes 7434240 | tf_op jit(solution)/shard_map/all_gather | solution.py:79
  124.7 10.5 %copy-start.1 = (s32[2,40]{1,0:T(2,128)S(1)}, s32[2,40]{1,0:T(2,128)}, u32[]{:S(2)}) copy-start(s32[2,40]{1,0:T(2,128)} %param.13) | copy-start | bytes 964
  128.2 41.8 %all-to-all-start = ((bf16[80,80,2,32]{0,3,2,1:T(8,128)(2,1)}), bf16[80,80,2,32]{0,3,2,1:T(8,128)(2,1)S(1)}, u32[]{:S(2)}, u32[]{:S(2)}) async-start(bf16[80,80,2,32]{0,3,2,1:T(8,128)(2,1)} %copy.32), calls=%async_computation | async-start | bytes 2621440 | tf_op jit(solution)/shard_map/all_to_all | solution.py:100
  594.0 39.9 %copy-start = (f32[40]{0:T(128)S(1)}, f32[40]{0:T(128)}, u32[]{:S(2)}) copy-start(f32[40]{0:T(128)} %param.12) | copy-start | bytes 484
  595.6 38.3 %all-to-all-start.1 = ((bf16[8,80,10,2,32]{1,4,3,2,0:T(8,128)(2,1)}), bf16[8,80,10,2,32]{1,4,3,2,0:T(8,128)(2,1)S(1)}, u32[]{:S(2)}, u32[]{:S(2)}) async-start(bf16[8,80,10,2,32]{1,4,3,2,0:T(8,128)(2,1)} %fusion.33), calls=%async_computation.1 | async-start | bytes 2621440 | tf_op jit(solution)/shard_map/all_to_all | solution.py:104
  599.2 190.0 %reduce-scatter.2.cloned.1.call-start = ((), (), s32[]{:S(2)}) async-start(), calls=%async_computation.4 | async-start | bytes 7434240 | tf_op jit(solution)/shard_map/reduce_scatter | solution.py:126
Sparse Core Ops, SparseCore 0:
  10.0 58.1 all-gather.1
  696.7 92.3 reduce-scatter.1
where the time goes:
time: 804 us; the launch traced here: 796 us
  matrix products  460 us (57%)
  waiting for transfers between devices  220 us (27%)
  local copies, waits for them, and re-layouts  68.9 us (9%)
  other arithmetic  22.8 us (3%)
  between operations  13.9 us (2%)
  starting transfers between devices  10.6 us (1%)
    dot_general x1, matrix products, fourier_work(): jnp.einsum('lfk,psk->plsf', products, sines, preferred_element_type=jnp.f...  108 us
    dot_general x1, matrix products, fourier_work(): jnp.einsum('plsf,psk->lfk', imag_part, sines, preferred_element_type=jnp....  104 us
    dot_general x1, matrix products, fourier_work(): jnp.einsum('plsf,psk->lfk', real_part, cosines, preferred_element_type=jn...  103 us
    dot_general x1, matrix products, fourier_work(): jnp.einsum('lfk,psk->plsf', products, cosines, preferred_element_type=jnp...  103 us
    reduce_scatter x1, waiting for transfers between devices, local(): lax.psum_scatter(jnp.moveaxis(picked_tiles, 0, 1).reshape(local_channels...  92.5 us
    all_gather x1, waiting for transfers between devices, local(): gathered = lax.all_gather(spec_in, 'lev', axis=0, tiled=True)  57.7 us
    while x20, matrix products  41.2 us
    all_to_all x1, waiting for transfers between devices, local(): lax.all_to_all(answered, 'lat', split_axis=0, concat_axis=0, tiled=True)  34.7 us
  transfers between devices with their start and end apart: 4, of which 4 were waited for; matrix products, arithmetic and copies ran while one was open for 0% of the time, Pallas kernels for 0%

commit v1 on v0

--- a/solution.py
+++ b/solution.py
@@ -97,7 +97,9 @@
     cosines, sines, wavenumbers = wave_tables(pair_count * groups, truncation)
     local_rows = row_points.reshape(1, 2 * lat_count)
     band_lats = 2 * lat_count // groups
-    lat_rows = lax.all_to_all(fourier, "lat", split_axis=1, concat_axis=0, tiled=True)
+    v_now = jnp.split(fourier, lax.psum(1, "lat"), axis=1)
+    placed = lax.all_to_all(jnp.stack(v_now), "lat", 0, 0)
+    lat_rows = jnp.concatenate(placed, axis=0)
     my_rows = lax.dynamic_slice_in_dim(local_rows[0], lax.axis_index("lat") * band_lats, band_lats)
     answered = fourier_work(lat_rows, my_rows, cosines, sines, wavenumbers, truncation)
     answered = answered.reshape(groups, pair_count, band_lats, 2, channels)

time: 804 us -> 831 us (1.034)
  local copies, waits for them, and re-layouts: 68.9 us -> 98.4 us
    another operation x0 -> x9, local copies, waits for them, and re-layouts: none -> 22.7 us  [local(): placed = lax.all_to_all(jnp.stack(v_now), 'lat', 0, 0)]
where the time goes in v1:
time: 831 us; the launch traced here: 825 us
  matrix products  459 us (55%)
  waiting for transfers between devices  220 us (26%)
  local copies, waits for them, and re-layouts  98.4 us (12%)
  other arithmetic  22 us (3%)
  between operations  14.2 us (2%)
  starting transfers between devices  10.6 us (1%)
    dot_general x1, matrix products, fourier_work(): jnp.einsum('lfk,psk->plsf', products, sines, preferred_element_type=jnp.f...  108 us
    dot_general x1, matrix products, fourier_work(): jnp.einsum('plsf,psk->lfk', imag_part, sines, preferred_element_type=jnp....  104 us
    dot_general x1, matrix products, fourier_work(): jnp.einsum('plsf,psk->lfk', real_part, cosines, preferred_element_type=jn...  103 us
    dot_general x1, matrix products, fourier_work(): jnp.einsum('lfk,psk->plsf', products, cosines, preferred_element_type=jnp...  103 us
    reduce_scatter x1, waiting for transfers between devices, local(): lax.psum_scatter(jnp.moveaxis(picked_tiles, 0, 1).reshape(local_channels...  92.7 us
    all_gather x1, waiting for transfers between devices, local(): gathered = lax.all_gather(spec_in, 'lev', axis=0, tiled=True)  57.7 us
    while x20, matrix products  41.2 us
    all_to_all x1, waiting for transfers between devices, local(): lax.all_to_all(answered, 'lat', split_axis=0, concat_axis=0, tiled=True)  34.7 us
  transfers between devices with their start and end apart: 4, of which 4 were waited for; matrix products, arithmetic and copies ran while one was open for 0% of the time, Pallas kernels for 0%

profile of v1, /device:TPU:2, one launch (start us, length us, event | category | flops | bytes accessed | tf_op | source)
XLA Modules:
  0.0 825.4 jit_solution(10463734065259561108)
XLA Ops:
  7.7 2.7 fusion.74
  10.4 57.7 %all-gather.2.cloned.1.call-done = bf16[32,80,1281]{2,1,0:T(8,128)(2,1)} async-done(((bf16[1,80,1281]{2,1,0:T(8,128)(2,1)}), bf16[32,80,1281]{2,1,0:T(8,128)(2,1)}) %all-gather.2.cloned.1.call-update) | async-done | bytes 6558736 | tf_op jit(solution)/shard_map/all_gather | solution.py:79
  68.2 7.4 copy.54
  75.6 45.1 %while.20 = (s32[]{:T(128)}, f32[10,8,40,4,32]{2,4,3,1,0:T(8,128)}, bf16[10,8,40,1281]{3,2,1,0:T(8,128)(2,1)}, bf16[10,32,8,1281]{3,1,2,0:T(8,128)(2,1)}, bf16[10,8,1281,4]{2,3,1,0:T(4,128)(2,1)S(1)}, /*index=5*/s32[]{:T(128)}) while((s32[]{:T(128)}, f32[10,8,40,4,32]{2,4,3,1,0:T(8,128)}, bf16[10,8,40,1281]{3,2,1,0:T(8,128)(2,1)}, ...), condition=%wide.region_1.2_spmd, body=%wide.region_0.1_spmd.sunk | while | flops 106251264 | bytes 9575181 | solution.py:90
  75.6 1.2 dynamic-slice_bitcast_fusion.7
  77.2 2.1 fusion.111
  80.1 1.2 dynamic-slice_bitcast_fusion.7
  81.7 2.1 fusion.111
  84.6 1.2 dynamic-slice_bitcast_fusion.7
  86.2 2.1 fusion.111
  89.1 1.2 dynamic-slice_bitcast_fusion.7
  90.7 2.1 fusion.111
  93.6 1.2 dynamic-slice_bitcast_fusion.7
  95.1 2.1 fusion.111
  98.1 1.2 dynamic-slice_bitcast_fusion.7
  99.6 2.1 fusion.111
  102.5 1.2 dynamic-slice_bitcast_fusion.7
  104.1 2.1 fusion.111
  107.0 1.2 dynamic-slice_bitcast_fusion.7
  108.6 2.1 fusion.111
  111.5 1.2 dynamic-slice_bitcast_fusion.7
  113.1 2.1 fusion.111
  116.0 1.2 dynamic-slice_bitcast_fusion.7
  117.6 2.1 fusion.111
  120.7 3.3 subtract_convert_fusion
  124.0 3.1 slice_bitcast_fusion.3
  127.1 2.9 copy.35
  130.7 2.9 copy.36
  133.6 2.9 copy.37
  136.5 1.6 copy.38
  138.1 3.1 fusion.76
  141.2 3.7 copy.39
  144.8 3.4 copy.40
  148.2 1.6 copy.41
  149.8 1.6 copy.34
  153.5 1.6 constant_dynamic-update-slice_fusion.3
  157.1 7.0 all-to-all-start
  164.6 34.4 %all-to-all-done = bf16[8,80,10,2,32]{1,4,3,2,0:T(8,128)(2,1)S(1)} async-done(((bf16[8,80,10,2,32]{1,4,3,2,0:T(8,128)(2,1)}), bf16[8,80,10,2,32]{1,4,3,2,0:T(8,128)(2,1)S(1)}, u32[]{:S(2)}, u32[]{:S(2)}) %all-to-all-start) | async-done | bytes 819232 | tf_op jit(solution)/shard_map/all_to_all | solution.py:101
  198.9 1.0 copy.42
  199.9 1.0 reshape.161
  201.1 103.7 %fusion.27 = f32[10,16,5120]{2,1,0:T(8,128)S(1)} fusion(s32[640,2]{0,1:T(2,128)S(1)} %get-tuple-element.98, bf16[640,10,2,16]{0,3,2,1:T(8,128)(2,1)S(1)} %fusion.97), kind=kOutput, calls=%fused_computation.38 | convolution fusion | flops 2162688000 | bytes 3691520 | tf_op jit(solution)/shard_map/plsf,psk->lfk/dot_general | solution.py:45
  304.8 103.3 %fusion.30 = f32[10,16,5120]{2,1,0:T(8,128)S(1)} fusion(f32[10,16,5120]{2,1,0:T(8,128)S(1)} %fusion.27, s32[640,2]{0,1:T(2,128)S(1)} %get-tuple-element.98, bf16[640,10,2,16]{0,3,2,1:T(8,128)(2,1)S(1)} %fusion.99), kind=kOutput, calls=%fused_computation.39 | convolution fusion | flops 2164326400 | bytes 6968320 | tf_op jit(solution)/shard_map/plsf,psk->lfk/dot_general | solution.py:40
  408.7 1.3 maximum_bitcast_fusion.10
  410.0 103.2 %fusion.41 = f32[640,10,2,16]{0,3,1,2:T(8,128)S(1)} fusion(s32[640,2]{0,1:T(2,128)S(1)} %get-tuple-element.98, bf16[10,16,5120,1]{2,1,0,3:T(8,128)(2,1)S(1)} %maximum_bitcast_fusion.9), kind=kOutput, calls=%fused_computation.63 | convolution fusion | flops 2162892800 | bytes 2462720 | tf_op jit(solution)/shard_map/lfk,psk->plsf/dot_general | solution.py:54
  514.0 107.7 %fusion.50 = f32[640,10,2,16]{0,3,1,2:T(8,128)S(1)} fusion(s32[640,2]{0,1:T(2,128)S(1)} %get-tuple-element.98, bf16[10,16,5120,1]{2,1,0,3:T(8,128)(2,1)} %maximum_bitcast_fusion.10), kind=kOutput, calls=%fused_computation.66 | convolution fusion | flops 2163097600 | bytes 2462720 | tf_op jit(solution)/shard_map/lfk,psk->plsf/dot_general | solution.py:58
  622.6 1.6 fusion.33
  624.2 3.6 all-to-all-start.1
  627.8 34.7 %all-to-all-done.1 = bf16[8,80,10,2,32]{1,4,3,2,0:T(8,128)(2,1)S(1)} async-done(((bf16[8,80,10,2,32]{1,4,3,2,0:T(8,128)(2,1)}), bf16[8,80,10,2,32]{1,4,3,2,0:T(8,128)(2,1)S(1)}, u32[]{:S(2)}, u32[]{:S(2)}) %all-to-all-start.1) | async-done | bytes 819232 | tf_op jit(solution)/shard_map/all_to_all | solution.py:106
  662.9 1.4 pad_maximum_fusion
  664.4 6.0 copy.45
  670.4 46.5 %while.21 = (s32[]{:T(128)}, bf16[10,32,8,1281]{3,1,2,0:T(8,128)(2,1)}, bf16[10,8,40,1281]{3,2,1,0:T(8,128)(2,1)}, bf16[10,8,40,4,32]{2,4,3,1,0:T(8,128)(2,1)S(1)}, f32[10,8,1281,4]{2,3,1,0:T(4,128)}, /*index=5*/s32[]{:T(128)}) while((s32[]{:T(128)}, bf16[10,32,8,1281]{3,1,2,0:T(8,128)(2,1)}, bf16[10,8,40,1281]{3,2,1,0:T(8,128)(2,1)}, ...), condition=%wide.region_4.5_spmd, body=%wide.region_2.4_spmd.sunk | while | flops 107235072 | bytes 14686669 | solution.py:127
  670.4 2.1 fusion.114
  675.0 2.1 fusion.114
  679.7 2.1 fusion.114
  684.4 2.1 fusion.114
  689.0 2.1 fusion.114
  693.6 2.1 fusion.114
  698.3 2.1 fusion.114
  702.9 2.1 fusion.114
  706.6 1.0 bitcast_dynamic-update-slice_fusion.3
  707.6 2.1 fusion.114
  712.2 2.1 fusion.114
  716.8 8.4 %copy.53 = bf16[32,10,8,1281]{3,2,1,0:T(8,128)(2,1)} copy(bf16[32,10,8,1281]{3,0,2,1:T(8,128)(2,1)} %bitcast.123) | data formatting | bytes 13117440 | tf_op jit(solution)/shard_map/convert_element_type | solution.py:131
  725.3 92.7 %reduce-scatter.2.cloned.1.call-done = bf16[1,80,1281]{2,1,0:T(8,128)(2,1)} async-done(((bf16[32,80,1281]{2,1,0:T(8,128)(2,1)}), bf16[1,80,1281]{2,1,0:T(8,128)(2,1)}) %reduce-scatter.2.cloned.1.call-update) | async-done | bytes 204976 | tf_op jit(solution)/shard_map/reduce_scatter | solution.py:128
  (110 shorter events, 46.1 us)
Async XLA Ops:
  6.5 61.6 %all-gather.2.cloned.1.call-start = ((), (), s32[]{:S(2)}) async-start(), calls=%async_computation.3 | async-start | bytes 7434240 | tf_op jit(solution)/shard_map/all_gather | solution.py:79
  141.2 7.0 copy-start
  149.8 14.3 %copy-start.2 = (s32[2,40]{1,0:T(2,128)S(1)}, s32[2,40]{1,0:T(2,128)}, u32[]{:S(2)}) copy-start(s32[2,40]{1,0:T(2,128)} %param.13) | copy-start | bytes 964
  157.1 41.8 %all-to-all-start = ((bf16[8,80,10,2,32]{1,4,3,2,0:T(8,128)(2,1)}), bf16[8,80,10,2,32]{1,4,3,2,0:T(8,128)(2,1)S(1)}, u32[]{:S(2)}, u32[]{:S(2)}) async-start(bf16[8,80,10,2,32]{1,4,3,2,0:T(8,128)(2,1)} %bitcast_dynamic-update-slice_fusion.1), calls=%async_computation | async-start | bytes 2621440 | tf_op jit(solution)/shard_map/all_to_all | solution.py:101
  622.6 39.9 %copy-start.1 = (f32[40]{0:T(128)S(1)}, f32[40]{0:T(128)}, u32[]{:S(2)}) copy-start(f32[40]{0:T(128)} %param.12) | copy-start | bytes 484
  624.2 38.3 %all-to-all-start.1 = ((bf16[8,80,10,2,32]{1,4,3,2,0:T(8,128)(2,1)}), bf16[8,80,10,2,32]{1,4,3,2,0:T(8,128)(2,1)S(1)}, u32[]{:S(2)}, u32[]{:S(2)}) async-start(bf16[8,80,10,2,32]{1,4,3,2,0:T(8,128)(2,1)} %fusion.33), calls=%async_computation.1 | async-start | bytes 2621440 | tf_op jit(solution)/shard_map/all_to_all | solution.py:106
  627.8 190.2 %reduce-scatter.2.cloned.1.call-start = ((), (), s32[]{:S(2)}) async-start(), calls=%async_computation.4 | async-start | bytes 7434240 | tf_op jit(solution)/shard_map/reduce_scatter | solution.py:128
Sparse Core Ops, SparseCore 0:
  10.0 58.1 all-gather.1
  725.4 92.5 reduce-scatter.1
